TPU v7x, 128 devices: a whole 4x4x4 slice. The times are simulated.
128 devices in a mesh: dp: 4 (over z), outer: 16 (over x, y), inner: 2 (over core).
Axes of the slice: x: 4, y: 4, z: 4, core: 2. Of those that a mesh axis runs over, the one named last changes fastest.
Arguments:
- tokens: bfloat16 [4096, 4096], P(('dp', 'outer', 'inner')), may hold values from -6 to 6
- expert_ids: int32 [4096, 8], P(('dp', 'outer', 'inner')), may hold values from 0 to 31, all different within a row; in each aligned block of 32 rows (0 to 31, 32 to 63, ...) at most 12 rows name the same one
- gate_values: float32 [4096, 8], P(('dp', 'outer', 'inner')), may hold values from 0.02 to 0.5
- upstream: bfloat16 [4096, 4096], P(('dp', 'outer', 'inner')), may hold values from -1.5 to 1.5
- w_gate: bfloat16 [32, 4096, 768], P(('outer', 'inner')), may hold values from -0.09375 to 0.09375
- w_up: bfloat16 [32, 4096, 768], P(('outer', 'inner')), may hold values from -0.09375 to 0.09375
- w_down: bfloat16 [32, 768, 4096], P(('outer', 'inner')), may hold values from -0.21875 to 0.21875
Outputs:
- output: bfloat16 [4096, 4096], P(('dp', 'outer', 'inner'))
- grad_tokens: bfloat16 [4096, 4096], P(('dp', 'outer', 'inner'))
- grad_gates: float32 [4096, 8], P(('dp', 'outer', 'inner'))
- grad_w_gate: bfloat16 [32, 4096, 768], P(('outer', 'inner'), 'dp')
- grad_w_up: bfloat16 [32, 4096, 768], P(('outer', 'inner'), 'dp')
- grad_w_down: bfloat16 [32, 768, 4096], P(('outer', 'inner'), None, 'dp')
Inputs may be any that keep to these rules, and one draw needn't show every extreme that they name: `expert_ids`: each token names 8 different experts. Among the 32 tokens of one device (aligned blocks of rows), no expert is named more than 12 times, a bound that some block reaches.
All inputs are finite; a program needn't handle non-finite values.
Results may differ from a plain program's by a relative error of at most 0.013.
Values may be sent and summed in bfloat16 or wider, within the bound.
No kernel may reach another device: no remote copies, remote signals or barrier semaphores. Data moves between devices by JAX's collectives and lax.ppermute only.
A program may use at most 192 MiB of HBM per device.

v0:
```python
import jax
import jax.numpy as jnp
from jax import lax
from jax.sharding import PartitionSpec as P


def contract_last(left, right):
    return lax.dot_general(
        left, right, (((1,), (1,)), ((), ())), preferred_element_type=jnp.float32
    )


def contract_first(left, right):
    return lax.dot_general(
        left, right, (((0,), (0,)), ((), ())), preferred_element_type=jnp.float32
    )


def expert_rows(rows_in, grads_in, gate_mat, up_mat, down_mat):
    gate_pre = jnp.dot(rows_in, gate_mat, preferred_element_type=jnp.float32)
    up_pre = jnp.dot(rows_in, up_mat, preferred_element_type=jnp.float32)
    sigma = jax.nn.sigmoid(gate_pre)
    silu_value = gate_pre * sigma
    hidden = (silu_value * up_pre).astype(jnp.bfloat16)
    expert_out = jnp.dot(hidden, down_mat, preferred_element_type=jnp.float32).astype(jnp.bfloat16)
    grad_hidden = contract_last(grads_in, down_mat)
    slope = sigma * (1.0 + gate_pre * (1.0 - sigma))
    grad_gate_pre = (grad_hidden * up_pre * slope).astype(jnp.bfloat16)
    grad_up_pre = (grad_hidden * silu_value).astype(jnp.bfloat16)
    pair_grad = (
        contract_last(grad_gate_pre, gate_mat) + contract_last(grad_up_pre, up_mat)
    ).astype(jnp.bfloat16)
    return (hidden, expert_out, grad_gate_pre, grad_up_pre, pair_grad)


def local(tokens, expert_ids, gate_values, upstream, w_gate, w_up, w_down):
    local_tokens = tokens.shape[0]
    width = tokens.shape[1]
    top_count = expert_ids.shape[1]
    ff_width = w_gate.shape[2]
    outer_count = lax.axis_size("outer")
    inner_count = lax.axis_size("inner")
    dp_count = lax.axis_size("dp")
    expert_count = outer_count * inner_count
    group = ("outer", "inner")
    me = lax.axis_index("outer") * inner_count + lax.axis_index("inner")
    group_tokens = expert_count * local_tokens
    capacity = min(local_tokens, 3 * local_tokens * top_count // (2 * expert_count))
    slot_total = expert_count * capacity
    ids_all = lax.all_gather(expert_ids, group, axis=0, tiled=True)
    gates_all = lax.all_gather(gate_values, group, axis=0, tiled=True)
    tokens_all = lax.all_gather(tokens, group, axis=0, tiled=True)
    upstream_all = lax.all_gather(upstream, group, axis=0, tiled=True)
    chosen = ids_all == me
    picked = jnp.any(chosen, axis=1)
    token_gate = jnp.sum(jnp.where(chosen, gates_all, 0.0), axis=1)
    position = jnp.cumsum(picked.astype(jnp.int32)) - 1
    token_slot = jnp.where(picked, position, slot_total)
    slot_token = (
        jnp.full((slot_total + 1,), group_tokens, jnp.int32)
        .at[token_slot]
        .set(jnp.arange(group_tokens, dtype=jnp.int32))[:slot_total]
    )
    token_pad = jnp.concatenate([tokens_all, jnp.zeros((1, width), jnp.bfloat16)], axis=0)
    upstream_pad = jnp.concatenate([upstream_all, jnp.zeros((1, width), jnp.bfloat16)], axis=0)
    gate_pad = jnp.concatenate([token_gate, jnp.zeros((1,), jnp.float32)], axis=0)
    rows_in = token_pad[slot_token]
    up_rows = upstream_pad[slot_token]
    grads_in = (gate_pad[slot_token][:, None] * up_rows.astype(jnp.float32)).astype(jnp.bfloat16)
    hidden, expert_out, grad_gate_pre, grad_up_pre, pair_grad = expert_rows(
        rows_in, grads_in, w_gate[0], w_up[0], w_down[0]
    )
    slot_gates_grad = jnp.sum(up_rows.astype(jnp.float32) * expert_out.astype(jnp.float32), axis=1)
    out_pad = jnp.concatenate([expert_out, jnp.zeros((1, width), jnp.bfloat16)], axis=0)
    back_pad = jnp.concatenate([pair_grad, jnp.zeros((1, width), jnp.bfloat16)], axis=0)
    gg_pad = jnp.concatenate([slot_gates_grad, jnp.zeros((1,), jnp.float32)], axis=0)
    out_share = (token_gate[:, None] * out_pad[token_slot].astype(jnp.float32)).astype(jnp.bfloat16)
    back_share = back_pad[token_slot]
    gg_share = jnp.where(chosen, gg_pad[token_slot][:, None], 0.0)
    output = lax.psum_scatter(out_share, group, scatter_dimension=0, tiled=True)
    grad_tokens = lax.psum_scatter(back_share, group, scatter_dimension=0, tiled=True)
    grad_gates = lax.psum_scatter(gg_share, group, scatter_dimension=0, tiled=True)
    piece = width // dp_count

    def spread_columns(block):
        return lax.all_to_all(
            block.reshape(slot_total, dp_count, piece),
            "dp",
            split_axis=1,
            concat_axis=0,
            tiled=True,
        ).reshape(dp_count * slot_total, piece)

    joined_grads = jnp.concatenate([grad_gate_pre, grad_up_pre], axis=1)
    rows_all = spread_columns(rows_in)
    grads_all = spread_columns(grads_in)
    joined_all = lax.all_gather(joined_grads, "dp", axis=0, tiled=True)
    hidden_all = lax.all_gather(hidden, "dp", axis=0, tiled=True)
    grad_joined = contract_first(rows_all, joined_all)
    grad_down = contract_first(hidden_all, grads_all)
    grad_w_gate = grad_joined[:, :ff_width].astype(jnp.bfloat16)[None]
    grad_w_up = grad_joined[:, ff_width:].astype(jnp.bfloat16)[None]
    grad_w_down = grad_down.astype(jnp.bfloat16)[None]
    return (output, grad_tokens, grad_gates, grad_w_gate, grad_w_up, grad_w_down)


def solution(mesh):
    placed = (
        P(("dp", "outer", "inner"), None),
        P(("dp", "outer", "inner"), None),
        P(("dp", "outer", "inner"), None),
        P(("dp", "outer", "inner"), None),
        P(("outer", "inner"), None, None),
        P(("outer", "inner"), None, None),
        P(("outer", "inner"), None, None),
    )
    return jax.shard_map(
        local,
        mesh=mesh,
        in_specs=placed,
        out_specs=(
            P(("dp", "outer", "inner"), None),
            P(("dp", "outer", "inner"), None),
            P(("dp", "outer", "inner"), None),
            P(("outer", "inner"), "dp", None),
            P(("outer", "inner"), "dp", None),
            P(("outer", "inner"), None, "dp"),
        ),
        check_vma=False,
    )
```

profile of v0, /device:TPU:0, one launch (start us, length us, event | category | flops | bytes accessed | tf_op | source)
XLA Modules:
  0.0 559.8 jit_solution(16613166208065047491)
XLA Ops:
  8.7 25.0 %all-gather = s32[32,32,8]{1,2,0:T(8,128)S(1)} all-gather(s32[1,32,8]{1,2,0:T(8,128)} %bitcast.73), channel_id=1, replica_groups=mesh['dp'=4,'outer'=16,'inner'=2] {'outer','inner'}, dimensions={0}, use_global_device_ids=true | all-gather | bytes 33792 | tf_op jit(solution)/shard_map/all_gather | solution.py:50
  34.5 24.0 %all-gather.1 = f32[32,32,8]{1,2,0:T(8,128)S(1)} all-gather(f32[1,32,8]{1,2,0:T(8,128)} %bitcast.74), channel_id=1, replica_groups=mesh['dp'=4,'outer'=16,'inner'=2] {'outer','inner'}, dimensions={0}, use_global_device_ids=true | all-gather | bytes 33792 | tf_op jit(solution)/shard_map/all_gather | solution.py:51
  58.8 4.6 scatter_custom_fusion
  63.5 2.5 gather_fusion.2
  66.1 7.7 %concatenate.24 = bf16[1025,4096]{1,0:T(8,128)(2,1)} pad(bf16[1024,4096]{1,0:T(8,128)(2,1)} %all-gather.9.cloned.1.call-done, bf16[]{:T(256)} %constant.7.clone.1), padding=0_1x0_0 | pad | bytes 16785410 | tf_op jit(solution)/shard_map/concatenate | solution.py:65
  73.8 12.8 %gather_fusion.3 = bf16[384,4096]{1,0:T(8,128)(2,1)} fusion(bf16[1025,4096]{1,0:T(8,128)(2,1)} %concatenate.24, s32[1024]{0:T(1024)S(1)} %pad_clamp_fusion), kind=kCustom, calls=%fused_computation.3 | custom fusion | bytes 6292992 | tf_op jit(solution)/shard_map/gather | solution.py:68
  86.6 34.0 %all-gather.7.cloned.1.call-done = bf16[1024,4096]{1,0:T(8,128)(2,1)} async-done(((bf16[32,4096]{1,0:T(8,128)(2,1)}), bf16[1024,4096]{1,0:T(8,128)(2,1)}) %all-gather.7.cloned.1.call-update) | async-done | bytes 8388624 | tf_op jit(solution)/shard_map/all_gather | solution.py:52
  120.6 7.7 %concatenate.21 = bf16[1025,4096]{1,0:T(8,128)(2,1)} pad(bf16[1024,4096]{1,0:T(8,128)(2,1)} %all-gather.7.cloned.1.call-done, bf16[]{:T(256)} %constant.7.clone.1), padding=0_1x0_0 | pad | bytes 16785410 | tf_op jit(solution)/shard_map/concatenate | solution.py:64
  128.3 12.5 %gather_fusion = bf16[384,4096]{1,0:T(8,128)(2,1)S(1)} fusion(bf16[1025,4096]{1,0:T(8,128)(2,1)} %concatenate.21, s32[1024]{0:T(1024)S(1)} %pad_clamp_fusion), kind=kCustom, calls=%fused_computation | custom fusion | bytes 6292992 | tf_op jit(solution)/shard_map/gather | solution.py:67
  140.8 6.5 %fusion.7 = f32[384,768]{1,0:T(8,128)S(1)} fusion(bf16[384,4096]{1,0:T(8,128)(2,1)S(1)} %gather_fusion, bf16[1,4096,768]{2,1,0:T(8,128)(2,1)} %param.12), kind=kOutput, calls=%fused_computation.16 | convolution fusion | flops 2415919104 | bytes 10616832 | tf_op jit(solution)/shard_map/dot_general | solution.py:21
  147.4 5.6 %fusion.1 = f32[384,768]{1,0:T(8,128)S(1)} fusion(bf16[1,768,4096]{2,1,0:T(8,128)(2,1)} %param.13, bf16[384,4096]{1,0:T(8,128)(2,1)S(1)} %copy-done.2, f32[384]{0:T(512)S(1)} %gather_fusion.2), kind=kOutput, calls=%fused_computation.10 | convolution fusion | flops 2420637696 | bytes 10618368 | tf_op jit(solution)/shard_map/dot_general | solution.py:8
  153.1 7.0 %multiply_convert_fusion.4 = (bf16[384,768]{1,0:T(8,128)(2,1)}, bf16[384,768]{1,0:T(8,128)(2,1)}, bf16[384,768]{1,0:T(8,128)(2,1)}) fusion(f32[384,768]{1,0:T(8,128)S(1)} %fusion.1, f32[384,768]{1,0:T(8,128)S(1)} %fusion.7, bf16[384,4096]{1,0:T(8,128)(2,1)S(1)} %gather_fusion, bf16[1,4096,768]{2,1,0:T(8,128)(2,1)} %param.11), kind=kOutput, calls=%fused_computation.36 | convolution fusion | flops 2420342784 | bytes 13565952 | tf_op jit(solution)/shard_map/dot_general | solution.py:20
  160.1 8.2 %multiply_reduce_fusion = (f32[384]{0:T(512)S(1)}, bf16[384,4096]{1,0:T(8,128)(2,1)}) fusion(bf16[384,4096]{1,0:T(8,128)(2,1)} %gather_fusion.3, bf16[384,768]{1,0:T(8,128)(2,1)} %get-tuple-element.12, bf16[1,768,4096]{2,1,0:T(8,128)(2,1)} %param.13), kind=kOutput, calls=%fused_computation.22 | convolution fusion | flops 2423782912 | bytes 13174272 | tf_op jit(solution)/shard_map/dot_general | solution.py:25
  168.3 6.9 %gather_fusion.5 = f32[1024]{0:T(1024)S(1)} fusion(f32[385]{0:T(512)S(1)} %pad_maximum_fusion.2, s32[1024]{0:T(1024)S(1)} %broadcast_clamp_fusion), kind=kCustom, calls=%fused_computation.5 | custom fusion | bytes 12288 | tf_op jit(solution)/shard_map/gather | solution.py:79
  178.1 4.9 fusion.5
  183.0 7.3 %add_convert_fusion = bf16[384,4096]{1,0:T(8,128)(2,1)S(1)} fusion(f32[384,4096]{1,0:T(8,128)S(1)} %fusion.5, bf16[384,768]{1,0:T(8,128)(2,1)S(1)} %copy-done.4, bf16[1,4096,768]{2,1,0:T(8,128)(2,1)} %param.11), kind=kOutput, calls=%fused_computation.23 | convolution fusion | flops 2419064832 | bytes 16318464 | tf_op jit(solution)/shard_map/dot_general | solution.py:8
  190.6 7.8 %gather_fusion.4 = bf16[1024,4096]{1,0:T(8,128)(2,1)} fusion(bf16[385,4096]{1,0:T(8,128)(2,1)S(1)} %concatenate.25, s32[1024]{0:T(1024)S(1)} %broadcast_clamp_fusion), kind=kCustom, calls=%fused_computation.4 | custom fusion | bytes 16781312 | tf_op jit(solution)/shard_map/gather | solution.py:78
  198.4 2.2 concatenate.22
  200.6 7.8 %gather_fusion.1 = bf16[1024,4096]{1,0:T(8,128)(2,1)} fusion(bf16[385,4096]{1,0:T(8,128)(2,1)S(1)} %concatenate.22, s32[1024]{0:T(1024)S(1)} %broadcast_clamp_fusion), kind=kCustom, calls=%fused_computation.1 | custom fusion | bytes 16781312 | tf_op jit(solution)/shard_map/gather | solution.py:77
  208.4 10.0 %multiply_convert_fusion = bf16[1024,4096]{1,0:T(8,128)(2,1)} fusion(bf16[1024,4096]{1,0:T(8,128)(2,1)} %gather_fusion.1, f32[1024]{0:T(1024)S(1)} %select_reduce_fusion), kind=kLoop, calls=%fused_computation.7 | loop fusion | flops 12582912 | bytes 16781312 | tf_op jit(solution)/shard_map/convert_element_type | solution.py:77
  221.0 2.8 fusion
  223.8 4.9 all-to-all-start.1
  228.8 2.2 copy.31
  230.9 36.1 %all-to-all-done.1 = bf16[384,4,1024]{2,0,1:T(8,128)(2,1)} async-done(((bf16[384,4,1024]{2,0,1:T(8,128)(2,1)}), bf16[384,4,1024]{2,0,1:T(8,128)(2,1)}, u32[]{:S(2)}, u32[]{:S(2)}) %all-to-all-start.1) | async-done | bytes 3145760 | tf_op jit(solution)/shard_map/all_to_all | solution.py:86
  267.1 3.9 all-to-all-start
  272.4 27.9 %all-gather.13.cloned.1.call-done = bf16[1536,768]{1,0:T(8,128)(2,1)} async-done(((bf16[384,768]{1,0:T(8,128)(2,1)}), bf16[1536,768]{1,0:T(8,128)(2,1)}) %all-gather.13.cloned.1.call-update) | async-done | bytes 2359312 | tf_op jit(solution)/shard_map/all_gather | solution.py:98
  300.3 6.4 %fusion.20 = bf16[1,768,1024]{2,1,0:T(8,128)(2,1)} fusion(bf16[1536,768]{1,0:T(8,128)(2,1)} %all-gather.13.cloned.1.call-done, bf16[1536,1024]{1,0:T(8,128)(2,1)} %bitcast.14), kind=kOutput, calls=%fused_computation.33 | convolution fusion | flops 2416705536 | bytes 7077888 | tf_op jit(solution)/shard_map/dot_general | solution.py:14
  306.7 17.0 %all-to-all-done = bf16[384,4,1024]{2,0,1:T(8,128)(2,1)S(1)} async-done(((bf16[384,4,1024]{2,0,1:T(8,128)(2,1)}), bf16[384,4,1024]{2,0,1:T(8,128)(2,1)S(1)}, u32[]{:S(2)}, u32[]{:S(2)}) %all-to-all-start) | async-done | bytes 3145760 | tf_op jit(solution)/shard_map/all_to_all | solution.py:86
  323.7 35.8 %all-gather.11.cloned.1.call-done = bf16[1536,1536]{1,0:T(8,128)(2,1)} async-done(((bf16[384,1536]{1,0:T(8,128)(2,1)}), bf16[1536,1536]{1,0:T(8,128)(2,1)}) %all-gather.11.cloned.1.call-update) | async-done | bytes 4718608 | tf_op jit(solution)/shard_map/all_gather | solution.py:97
  359.5 7.7 %convolution_convert_fusion = bf16[1024,1536]{1,0:T(8,128)(2,1)S(1)} fusion(bf16[1536,1024]{1,0:T(8,128)(2,1)S(1)} %bitcast.69, bf16[1536,1536]{1,0:T(8,128)(2,1)} %all-gather.11.cloned.1.call-done), kind=kOutput, calls=%fused_computation.26 | convolution fusion | flops 4833411072 | bytes 11010048 | tf_op jit(solution)/shard_map/dot_general | solution.py:14
  369.1 86.9 %reduce-scatter.8.cloned.1.call-done = bf16[32,4096]{1,0:T(8,128)(2,1)} async-done(((bf16[1024,4096]{1,0:T(8,128)(2,1)}), bf16[32,4096]{1,0:T(8,128)(2,1)}) %reduce-scatter.8.cloned.1.call-update) | async-done | bytes 262160 | tf_op jit(solution)/shard_map/reduce_scatter | solution.py:81
  456.0 96.7 %reduce-scatter.6.cloned.1.call-done = bf16[32,4096]{1,0:T(8,128)(2,1)} async-done(((bf16[1024,4096]{1,0:T(8,128)(2,1)}), bf16[32,4096]{1,0:T(8,128)(2,1)}) %reduce-scatter.6.cloned.1.call-update) | async-done | bytes 262160 | tf_op jit(solution)/shard_map/reduce_scatter | solution.py:80
  (56 shorter events, 11.7 us)
Async XLA Ops:
  7.2 58.9 %all-gather.9.cloned.1.call-start = ((), (), s32[]{:S(2)}) async-start(), calls=%async_computation.7 | async-start | bytes 8650752 | tf_op jit(solution)/shard_map/all_gather | solution.py:53
  7.9 112.7 %all-gather.7.cloned.1.call-start = ((), (), s32[]{:S(2)}) async-start(), calls=%async_computation.5 | async-start | bytes 8650752 | tf_op jit(solution)/shard_map/all_gather | solution.py:52
  8.6 262.4 %reduce-scatter.10.cloned.1.call-start = ((), (), s32[]{:S(2)}) async-start(), calls=%async_computation.11 | async-start | bytes 540672
  140.8 12.2 %copy-start = (bf16[384,4096]{1,0:T(8,128)(2,1)}, bf16[384,4096]{1,0:T(8,128)(2,1)S(1)}, u32[]{:S(2)}) copy-start(bf16[384,4096]{1,0:T(8,128)(2,1)S(1)} %gather_fusion) | copy-start | bytes 9437188
  140.8 6.6 %copy-start.2 = (bf16[384,4096]{1,0:T(8,128)(2,1)S(1)}, bf16[384,4096]{1,0:T(8,128)(2,1)}, u32[]{:S(2)}) copy-start(bf16[384,4096]{1,0:T(8,128)(2,1)} %gather_fusion.3) | copy-start | bytes 9437188
  168.3 8.6 %copy-start.4 = (bf16[384,768]{1,0:T(8,128)(2,1)S(1)}, bf16[384,768]{1,0:T(8,128)(2,1)}, u32[]{:S(2)}) copy-start(bf16[384,768]{1,0:T(8,128)(2,1)} %get-tuple-element.10) | copy-start | bytes 1769476
  168.3 8.6 %copy-start.5 = (bf16[384,768]{1,0:T(8,128)(2,1)S(1)}, bf16[384,768]{1,0:T(8,128)(2,1)}, u32[]{:S(2)}) copy-start(bf16[384,768]{1,0:T(8,128)(2,1)} %get-tuple-element.11) | copy-start | bytes 1769476
  176.2 124.1 %all-gather.13.cloned.1.call-start = ((), (), s32[]{:S(2)}) async-start(), calls=%async_computation.10 | async-start | bytes 2949120 | tf_op jit(solution)/shard_map/all_gather | solution.py:98
  176.8 182.7 %all-gather.11.cloned.1.call-start = ((), (), s32[]{:S(2)}) async-start(), calls=%async_computation.9 | async-start | bytes 5898240 | tf_op jit(solution)/shard_map/all_gather | solution.py:97
  178.0 278.0 %reduce-scatter.8.cloned.1.call-start = ((), (), s32[]{:S(2)}) async-start(), calls=%async_computation.8 | async-start | bytes 8650752 | tf_op jit(solution)/shard_map/reduce_scatter | solution.py:81
  198.4 354.4 %reduce-scatter.6.cloned.1.call-start = ((), (), s32[]{:S(2)}) async-start(), calls=%async_computation.6 | async-start | bytes 8650752 | tf_op jit(solution)/shard_map/reduce_scatter | solution.py:80
  218.4 1.9 copy-start.3
  223.8 5.0 copy-start.1
  223.8 43.3 %all-to-all-start.1 = ((bf16[384,4,1024]{2,0,1:T(8,128)(2,1)}), bf16[384,4,1024]{2,0,1:T(8,128)(2,1)}, u32[]{:S(2)}, u32[]{:S(2)}) async-start(bf16[384,4,1024]{2,0,1:T(8,128)(2,1)} %fusion), calls=%async_computation.3 | async-start | bytes 6291456 | tf_op jit(solution)/shard_map/all_to_all | solution.py:86
  267.1 56.6 %all-to-all-start = ((bf16[384,4,1024]{2,0,1:T(8,128)(2,1)}), bf16[384,4,1024]{2,0,1:T(8,128)(2,1)S(1)}, u32[]{:S(2)}, u32[]{:S(2)}) async-start(bf16[384,4,1024]{2,0,1:T(8,128)(2,1)} %bitcast.68), calls=%async_computation.2 | async-start | bytes 6291456 | tf_op jit(solution)/shard_map/all_to_all | solution.py:86
Sparse Core Ops, SparseCore 0:
  10.3 55.5 all-gather.8
  68.1 52.4 all-gather.6
  176.4 76.5 reduce-scatter.9
  255.0 45.2 all-gather.12
  302.4 57.0 all-gather.10
  363.7 92.2 reduce-scatter.7
  460.8 91.9 reduce-scatter.5
where the time goes:
time: 564 us; the launch traced here: 560 us
  waiting for transfers between devices  337 us (60%)
  local copies, waits for them, and re-layouts  81.7 us (14%)
  matrix products  53.7 us (10%)
  blocking collectives  49 us (9%)
  other arithmetic  15.1 us (3%)
  between operations  14.6 us (3%)
  starting transfers between devices  9.13 us (2%)
    reduce_scatter x1, waiting for transfers between devices, local(): output = lax.psum_scatter(out_share, group, scatter_dimension=0, tiled=True)  96.7 us
    reduce_scatter x1, waiting for transfers between devices, local(): lax.psum_scatter(back_share, group, scatter_dimension=0, tiled=True)  86.9 us
    all_to_all x2, waiting for transfers between devices, spread_columns(): lax.all_to_all(block.reshape(slot_total, dp_count, piece), 'dp', split_ax...  53.1 us
    all_gather x1, waiting for transfers between devices, local(): joined_all = lax.all_gather(joined_grads, 'dp', axis=0, tiled=True)  35.8 us
    all_gather x1, waiting for transfers between devices, local(): tokens_all = lax.all_gather(tokens, group, axis=0, tiled=True)  34 us
    all_gather x1, waiting for transfers between devices, local(): hidden_all = lax.all_gather(hidden, 'dp', axis=0, tiled=True)  27.9 us
    all_gather x1, blocking collectives, local(): ids_all = lax.all_gather(expert_ids, group, axis=0, tiled=True)  25 us
    all_gather x1, blocking collectives, local(): gates_all = lax.all_gather(gate_values, group, axis=0, tiled=True)  24 us
  transfers between devices with their start and end apart: 9, of which 7 were waited for; matrix products, arithmetic and copies ran while one was open for 17% of the time, Pallas kernels for 0%

commit v1 on v0

--- a/solution.py
+++ b/solution.py
@@ -2,6 +2,27 @@
 import jax.numpy as jnp
 from jax import lax
 from jax.sharding import PartitionSpec as P
+
+
+def gather_around(shard, axis, dim):
+    length, here, width = (lax.axis_size(axis), lax.axis_index(axis), shard.shape[dim])
+    right = [(i, (i + 1) % length) for i in range(length)]
+    behind = [(i, (i - 1) % length) for i in range(length)]
+    result = jnp.zeros((*shard.shape[:dim], length * width, *shard.shape[dim + 1 :]), shard.dtype)
+    result = lax.dynamic_update_slice_in_dim(result, shard, here * width, axis=dim)
+    from_left = from_right = shard
+    half = length // 2
+    for step in range(1, half + 1):
+        from_left = lax.ppermute(from_left, axis, right)
+        result = lax.dynamic_update_slice_in_dim(
+            result, from_left, (here - step) % length * width, axis=dim
+        )
+        if step < length - half:
+            from_right = lax.ppermute(from_right, axis, behind)
+            result = lax.dynamic_update_slice_in_dim(
+                result, from_right, (here + step) % length * width, axis=dim
+            )
+    return result
 
 
 def contract_last(left, right):
@@ -94,7 +115,7 @@
     joined_grads = jnp.concatenate([grad_gate_pre, grad_up_pre], axis=1)
     rows_all = spread_columns(rows_in)
     grads_all = spread_columns(grads_in)
-    joined_all = lax.all_gather(joined_grads, "dp", axis=0, tiled=True)
+    joined_all = gather_around(joined_grads, "dp", 0)
     hidden_all = lax.all_gather(hidden, "dp", axis=0, tiled=True)
     grad_joined = contract_first(rows_all, joined_all)
     grad_down = contract_first(hidden_all, grads_all)

time: 564 us -> 510 us (0.904)
  waiting for transfers between devices: 337 us -> 270 us
  local copies, waits for them, and re-layouts: 81.7 us -> 90.2 us
    ppermute x0 -> x3, waiting for transfers between devices: none -> 92 us  [the longest x2 92 us: gather_around(): from_left = lax.ppermute(from_left, axis, right)]
    reduce_scatter x1, waiting for transfers between devices: 86.9 us -> 25.8 us  [local(): lax.psum_scatter(back_share, group, scatter_dimension=0, tiled=True)]
    all_gather x1 -> x0, waiting for transfers between devices: 35.8 us -> none  [local(): joined_all = lax.all_gather(joined_grads, 'dp', axis=0, tiled=True)]
    all_to_all x2, waiting for transfers between devices: 53.1 us -> 19.6 us  [spread_columns(): lax.all_to_all(block.reshape(slot_total, dp_count, piece), 'dp', split_ax...]
    all_gather x1, waiting for transfers between devices: 27.9 us -> 0.01 us  [local(): hidden_all = lax.all_gather(hidden, 'dp', axis=0, tiled=True)]
    dynamic_update_slice x0 -> x3, local copies, waits for them, and re-layouts: none -> 7.26 us  [the longest x2 4.84 us: gather_around(): lax.dynamic_update_slice_in_dim(result, from_left, (here - step) % length...]
  transfers between devices with their start and end apart: 9 -> 11, of which waited for: 7 -> 6; matrix products, arithmetic and copies ran while one was open for 17% -> 20% of each run, Pallas kernels for 0% -> 0%
where the time goes in v1:
time: 510 us; the launch traced here: 506 us
  waiting for transfers between devices  270 us (53%)
  local copies, waits for them, and re-layouts  90.2 us (18%)
  matrix products  54 us (11%)
  blocking collectives  49 us (10%)
  other arithmetic  15.3 us (3%)
  between operations  14.7 us (3%)
  starting transfers between devices  12.8 us (3%)
    reduce_scatter x1, waiting for transfers between devices, local(): output = lax.psum_scatter(out_share, group, scatter_dimension=0, tiled=True)  96.6 us
    ppermute x2, waiting for transfers between devices, gather_around(): from_left = lax.ppermute(from_left, axis, right)  92 us
    all_gather x1, waiting for transfers between devices, local(): tokens_all = lax.all_gather(tokens, group, axis=0, tiled=True)  34 us
    reduce_scatter x1, waiting for transfers between devices, local(): lax.psum_scatter(back_share, group, scatter_dimension=0, tiled=True)  25.8 us
    all_gather x1, blocking collectives, local(): ids_all = lax.all_gather(expert_ids, group, axis=0, tiled=True)  25 us
    all_gather x1, blocking collectives, local(): gates_all = lax.all_gather(gate_values, group, axis=0, tiled=True)  24 us
    all_to_all x2, waiting for transfers between devices, spread_columns(): lax.all_to_all(block.reshape(slot_total, dp_count, piece), 'dp', split_ax...  19.6 us
    dot_general x3, matrix products, contract_last(): lax.dot_general(left, right, (((1,), (1,)), ((), ())), preferred_element_...  17.9 us
  transfers between devices with their start and end apart: 11, of which 6 were waited for; matrix products, arithmetic and copies ran while one was open for 20% of the time, Pallas kernels for 0%

profile of v1, /device:TPU:0, one launch (start us, length us, event | category | flops | bytes accessed | tf_op | source)
XLA Modules:
  0.0 506.0 jit_solution(10604069170392813584)
XLA Ops:
  8.7 25.0 %all-gather = s32[32,32,8]{1,2,0:T(8,128)S(1)} all-gather(s32[1,32,8]{1,2,0:T(8,128)} %bitcast.73), channel_id=1, replica_groups=mesh['dp'=4,'outer'=16,'inner'=2] {'outer','inner'}, dimensions={0}, use_global_device_ids=true | all-gather | bytes 33792 | tf_op jit(solution)/shard_map/all_gather | solution.py:71
  34.5 24.0 %all-gather.1 = f32[32,32,8]{1,2,0:T(8,128)S(1)} all-gather(f32[1,32,8]{1,2,0:T(8,128)} %bitcast.74), channel_id=1, replica_groups=mesh['dp'=4,'outer'=16,'inner'=2] {'outer','inner'}, dimensions={0}, use_global_device_ids=true | all-gather | bytes 33792 | tf_op jit(solution)/shard_map/all_gather | solution.py:72
  58.8 4.6 scatter_custom_fusion
  63.5 2.5 gather_fusion.2
  66.1 7.7 %concatenate.24 = bf16[1025,4096]{1,0:T(8,128)(2,1)} pad(bf16[1024,4096]{1,0:T(8,128)(2,1)} %all-gather.8.cloned.1.call-done, bf16[]{:T(256)} %constant.55.clone.1), padding=0_1x0_0 | pad | bytes 16785410 | tf_op jit(solution)/shard_map/concatenate | solution.py:86
  73.8 12.8 %gather_fusion.3 = bf16[384,4096]{1,0:T(8,128)(2,1)} fusion(bf16[1025,4096]{1,0:T(8,128)(2,1)} %concatenate.24, s32[1024]{0:T(1024)S(1)} %pad_clamp_fusion), kind=kCustom, calls=%fused_computation.3 | custom fusion | bytes 6292992 | tf_op jit(solution)/shard_map/gather | solution.py:89
  86.6 34.0 %all-gather.6.cloned.1.call-done = bf16[1024,4096]{1,0:T(8,128)(2,1)} async-done(((bf16[32,4096]{1,0:T(8,128)(2,1)}), bf16[1024,4096]{1,0:T(8,128)(2,1)}) %all-gather.6.cloned.1.call-update) | async-done | bytes 8388624 | tf_op jit(solution)/shard_map/all_gather | solution.py:73
  120.6 7.7 %concatenate.21 = bf16[1025,4096]{1,0:T(8,128)(2,1)} pad(bf16[1024,4096]{1,0:T(8,128)(2,1)} %all-gather.6.cloned.1.call-done, bf16[]{:T(256)} %constant.55.clone.1), padding=0_1x0_0 | pad | bytes 16785410 | tf_op jit(solution)/shard_map/concatenate | solution.py:85
  128.3 12.5 %gather_fusion = bf16[384,4096]{1,0:T(8,128)(2,1)S(1)} fusion(bf16[1025,4096]{1,0:T(8,128)(2,1)} %concatenate.21, s32[1024]{0:T(1024)S(1)} %pad_clamp_fusion), kind=kCustom, calls=%fused_computation | custom fusion | bytes 6292992 | tf_op jit(solution)/shard_map/gather | solution.py:88
  140.8 6.5 %fusion.7 = f32[384,768]{1,0:T(8,128)S(1)} fusion(bf16[384,4096]{1,0:T(8,128)(2,1)S(1)} %gather_fusion, bf16[1,4096,768]{2,1,0:T(8,128)(2,1)} %param.12), kind=kOutput, calls=%fused_computation.16 | convolution fusion | flops 2415919104 | bytes 10616832 | tf_op jit(solution)/shard_map/dot_general | solution.py:42
  147.4 5.6 %fusion.1 = f32[384,768]{1,0:T(8,128)S(1)} fusion(bf16[1,768,4096]{2,1,0:T(8,128)(2,1)} %param.13, bf16[384,4096]{1,0:T(8,128)(2,1)S(1)} %copy-done.2, f32[384]{0:T(512)S(1)} %gather_fusion.2), kind=kOutput, calls=%fused_computation.10 | convolution fusion | flops 2420637696 | bytes 10618368 | tf_op jit(solution)/shard_map/dot_general | solution.py:29
  153.1 7.0 %multiply_convert_fusion.4 = (bf16[384,768]{1,0:T(8,128)(2,1)}, bf16[384,768]{1,0:T(8,128)(2,1)}, bf16[384,768]{1,0:T(8,128)(2,1)}) fusion(f32[384,768]{1,0:T(8,128)S(1)} %fusion.1, f32[384,768]{1,0:T(8,128)S(1)} %fusion.7, bf16[384,4096]{1,0:T(8,128)(2,1)S(1)} %gather_fusion, bf16[1,4096,768]{2,1,0:T(8,128)(2,1)} %param.11), kind=kOutput, calls=%fused_computation.36 | convolution fusion | flops 2420342784 | bytes 13565952 | tf_op jit(solution)/shard_map/dot_general | solution.py:41
  160.1 8.2 %multiply_reduce_fusion = (f32[384]{0:T(512)S(1)}, bf16[384,4096]{1,0:T(8,128)(2,1)}) fusion(bf16[384,4096]{1,0:T(8,128)(2,1)} %gather_fusion.3, bf16[384,768]{1,0:T(8,128)(2,1)} %get-tuple-element.12, bf16[1,768,4096]{2,1,0:T(8,128)(2,1)} %param.13), kind=kOutput, calls=%fused_computation.22 | convolution fusion | flops 2423782912 | bytes 13174272 | tf_op jit(solution)/shard_map/dot_general | solution.py:46
  168.3 6.9 %gather_fusion.5 = f32[1024]{0:T(1024)S(1)} fusion(f32[385]{0:T(512)S(1)} %pad_maximum_fusion.2, s32[1024]{0:T(1024)S(1)} %broadcast_clamp_fusion), kind=kCustom, calls=%fused_computation.5 | custom fusion | bytes 12288 | tf_op jit(solution)/shard_map/gather | solution.py:100
  176.9 4.9 fusion.5
  181.8 7.3 %add_convert_fusion = bf16[384,4096]{1,0:T(8,128)(2,1)S(1)} fusion(f32[384,4096]{1,0:T(8,128)S(1)} %fusion.5, bf16[384,768]{1,0:T(8,128)(2,1)S(1)} %copy-done.5, bf16[1,4096,768]{2,1,0:T(8,128)(2,1)} %param.11), kind=kOutput, calls=%fused_computation.23 | convolution fusion | flops 2419064832 | bytes 16318464 | tf_op jit(solution)/shard_map/dot_general | solution.py:29
  189.4 7.8 %gather_fusion.4 = bf16[1024,4096]{1,0:T(8,128)(2,1)} fusion(bf16[385,4096]{1,0:T(8,128)(2,1)S(1)} %concatenate.25, s32[1024]{0:T(1024)S(1)} %broadcast_clamp_fusion), kind=kCustom, calls=%fused_computation.4 | custom fusion | bytes 16781312 | tf_op jit(solution)/shard_map/gather | solution.py:99
  199.4 7.8 %gather_fusion.1 = bf16[1024,4096]{1,0:T(8,128)(2,1)} fusion(bf16[385,4096]{1,0:T(8,128)(2,1)S(1)} %concatenate.22, s32[1024]{0:T(1024)S(1)} %broadcast_clamp_fusion), kind=kCustom, calls=%fused_computation.1 | custom fusion | bytes 16781312 | tf_op jit(solution)/shard_map/gather | solution.py:98
  207.2 10.0 %multiply_convert_fusion = bf16[1024,4096]{1,0:T(8,128)(2,1)} fusion(bf16[1024,4096]{1,0:T(8,128)(2,1)} %gather_fusion.1, f32[1024]{0:T(1024)S(1)} %select_reduce_fusion), kind=kLoop, calls=%fused_computation.7 | loop fusion | flops 12582912 | bytes 16781312 | tf_op jit(solution)/shard_map/convert_element_type | solution.py:98
  221.2 4.4 all-to-all-start
  231.4 76.4 %collective-permute-done = bf16[384,1536]{1,0:T(8,128)(2,1)} collective-permute-done((bf16[384,1536]{1,0:T(8,128)(2,1)}, bf16[384,1536]{1,0:T(8,128)(2,1)}, u32[]{:S(2)}, u32[]{:S(2)}) %collective-permute-start) | collective-permute-done | bytes 1179680 | tf_op jit(solution)/shard_map/ppermute | solution.py:16
  308.5 2.8 fusion
  311.3 4.9 all-to-all-start.1
  317.6 2.4 constant_dynamic-update-slice_fusion.2
  320.0 2.4 constant_dynamic-update-slice_fusion.1
  322.5 15.7 %collective-permute-done.2 = bf16[384,1536]{1,0:T(8,128)(2,1)} collective-permute-done((bf16[384,1536]{1,0:T(8,128)(2,1)}, bf16[384,1536]{1,0:T(8,128)(2,1)}, u32[]{:S(2)}, u32[]{:S(2)}) %collective-permute-start.2) | collective-permute-done | bytes 1179680 | tf_op jit(solution)/shard_map/ppermute | solution.py:16
  338.1 2.5 constant_dynamic-update-slice_fusion
  340.6 7.9 %convolution_convert_fusion = bf16[1024,1536]{1,0:T(8,128)(2,1)S(1)} fusion(bf16[1536,1024]{1,0:T(8,128)(2,1)S(1)} %bitcast.69, bf16[1536,1536]{1,0:T(8,128)(2,1)} %constant_dynamic-update-slice_fusion), kind=kOutput, calls=%fused_computation.26 | convolution fusion | flops 4833411072 | bytes 11010048 | tf_op jit(solution)/shard_map/dot_general | solution.py:35
  350.4 19.6 %all-to-all-done.1 = bf16[384,4,1024]{2,0,1:T(8,128)(2,1)} async-done(((bf16[384,4,1024]{2,0,1:T(8,128)(2,1)}), bf16[384,4,1024]{2,0,1:T(8,128)(2,1)}, u32[]{:S(2)}, u32[]{:S(2)}) %all-to-all-start.1) | async-done | bytes 3145760 | tf_op jit(solution)/shard_map/all_to_all | solution.py:107
  369.9 6.5 %fusion.20 = bf16[1,768,1024]{2,1,0:T(8,128)(2,1)} fusion(bf16[1536,768]{1,0:T(8,128)(2,1)} %all-gather.10.cloned.1.call-done, bf16[1536,1024]{1,0:T(8,128)(2,1)} %bitcast.14), kind=kOutput, calls=%fused_computation.33 | convolution fusion | flops 2416705536 | bytes 7077888 | tf_op jit(solution)/shard_map/dot_general | solution.py:35
  376.5 25.8 %reduce-scatter.8.cloned.1.call-done = bf16[32,4096]{1,0:T(8,128)(2,1)} async-done(((bf16[1024,4096]{1,0:T(8,128)(2,1)}), bf16[32,4096]{1,0:T(8,128)(2,1)}) %reduce-scatter.8.cloned.1.call-update) | async-done | bytes 262160 | tf_op jit(solution)/shard_map/reduce_scatter | solution.py:102
  402.3 96.6 %reduce-scatter.6.cloned.1.call-done = bf16[32,4096]{1,0:T(8,128)(2,1)} async-done(((bf16[1024,4096]{1,0:T(8,128)(2,1)}), bf16[32,4096]{1,0:T(8,128)(2,1)}) %reduce-scatter.6.cloned.1.call-update) | async-done | bytes 262160 | tf_op jit(solution)/shard_map/reduce_scatter | solution.py:101
  (69 shorter events, 20.5 us)
Async XLA Ops:
  7.2 58.9 %all-gather.8.cloned.1.call-start = ((), (), s32[]{:S(2)}) async-start(), calls=%async_computation.7 | async-start | bytes 8650752 | tf_op jit(solution)/shard_map/all_gather | solution.py:74
  7.9 112.7 %all-gather.6.cloned.1.call-start = ((), (), s32[]{:S(2)}) async-start(), calls=%async_computation.5 | async-start | bytes 8650752 | tf_op jit(solution)/shard_map/all_gather | solution.py:73
  8.6 307.6 %reduce-scatter.10.cloned.1.call-start = ((), (), s32[]{:S(2)}) async-start(), calls=%async_computation.10 | async-start | bytes 540672
  140.8 12.2 %copy-start = (bf16[384,4096]{1,0:T(8,128)(2,1)}, bf16[384,4096]{1,0:T(8,128)(2,1)S(1)}, u32[]{:S(2)}) copy-start(bf16[384,4096]{1,0:T(8,128)(2,1)S(1)} %gather_fusion) | copy-start | bytes 9437188
  140.8 6.6 %copy-start.2 = (bf16[384,4096]{1,0:T(8,128)(2,1)S(1)}, bf16[384,4096]{1,0:T(8,128)(2,1)}, u32[]{:S(2)}) copy-start(bf16[384,4096]{1,0:T(8,128)(2,1)} %gather_fusion.3) | copy-start | bytes 9437188
  168.3 8.6 %copy-start.7 = (bf16[384,768]{1,0:T(8,128)(2,1)S(1)}, bf16[384,768]{1,0:T(8,128)(2,1)}, u32[]{:S(2)}) copy-start(bf16[384,768]{1,0:T(8,128)(2,1)} %get-tuple-element.11) | copy-start | bytes 1769476
  176.2 193.7 %all-gather.10.cloned.1.call-start = ((), (), s32[]{:S(2)}) async-start(), calls=%async_computation.9 | async-start | bytes 2949120 | tf_op jit(solution)/shard_map/all_gather | solution.py:119
  176.8 225.5 %reduce-scatter.8.cloned.1.call-start = ((), (), s32[]{:S(2)}) async-start(), calls=%async_computation.8 | async-start | bytes 8650752 | tf_op jit(solution)/shard_map/reduce_scatter | solution.py:102
  176.9 5.0 copy-start.5
  197.2 301.7 %reduce-scatter.6.cloned.1.call-start = ((), (), s32[]{:S(2)}) async-start(), calls=%async_computation.6 | async-start | bytes 8650752 | tf_op jit(solution)/shard_map/reduce_scatter | solution.py:101
  217.2 1.9 copy-start.1
  221.2 90.0 %all-to-all-start = ((bf16[384,4,1024]{2,0,1:T(8,128)(2,1)}), bf16[384,4,1024]{2,0,1:T(8,128)(2,1)S(1)}, u32[]{:S(2)}, u32[]{:S(2)}) async-start(bf16[384,4,1024]{2,0,1:T(8,128)(2,1)} %bitcast.68), calls=%async_computation.2 | async-start | bytes 6291456 | tf_op jit(solution)/shard_map/all_to_all | solution.py:107
  225.7 1.1 copy-start.6
  225.7 1.2 copy-start.8
  225.7 82.0 %copy-start.3 = (bf16[384,4096]{1,0:T(8,128)(2,1)S(1)}, bf16[384,4096]{1,0:T(8,128)(2,1)}, u32[]{:S(2)}) copy-start(bf16[384,4096]{1,0:T(8,128)(2,1)} %gather_fusion.3) | copy-start | bytes 9437188
  228.1 79.6 %copy-start.4 = (bf16[1536,1536]{1,0:T(8,128)(2,1)}, bf16[1536,1536]{1,0:T(8,128)(2,1)S(1)}, u32[]{:S(2)}) copy-start(bf16[1536,1536]{1,0:T(8,128)(2,1)S(1)} %get-tuple-element.14) | copy-start | bytes 14155780
  228.1 79.6 %collective-permute-start = (bf16[384,1536]{1,0:T(8,128)(2,1)}, bf16[384,1536]{1,0:T(8,128)(2,1)}, u32[]{:S(2)}, u32[]{:S(2)}) collective-permute-start(bf16[384,1536]{1,0:T(8,128)(2,1)} %get-tuple-element.13), channel_id=1, source_target_pairs={{0,32},{32,64},{64,96},{96,0},{1,33},{33,65},{65,97},{97,1},{2,34}... | collective-permute-start | bytes 3538952 | tf_op jit(solution)/shard_map/ppermute | solution.py:16
  230.1 89.9 %collective-permute-start.1 = (bf16[384,1536]{1,0:T(8,128)(2,1)}, bf16[384,1536]{1,0:T(8,128)(2,1)}, u32[]{:S(2)}, u32[]{:S(2)}) collective-permute-start(bf16[384,1536]{1,0:T(8,128)(2,1)} %get-tuple-element.13), channel_id=1, source_target_pairs={{0,96},{32,0},{64,32},{96,64},{1,97},{33,1},{65,33},{97,65},{2,98}... | collective-permute-start | bytes 3538952 | tf_op jit(solution)/shard_map/ppermute | solution.py:21
  307.7 30.4 %collective-permute-start.2 = (bf16[384,1536]{1,0:T(8,128)(2,1)}, bf16[384,1536]{1,0:T(8,128)(2,1)}, u32[]{:S(2)}, u32[]{:S(2)}) collective-permute-start(bf16[384,1536]{1,0:T(8,128)(2,1)} %collective-permute-done), channel_id=1, source_target_pairs={{0,32},{32,64},{64,96},{96,0},{1,33},{33,65},{65,97},{97,1},{2,34}... | collective-permute-start | bytes 3538952 | tf_op jit(solution)/shard_map/ppermute | solution.py:16
  311.3 58.6 %all-to-all-start.1 = ((bf16[384,4,1024]{2,0,1:T(8,128)(2,1)}), bf16[384,4,1024]{2,0,1:T(8,128)(2,1)}, u32[]{:S(2)}, u32[]{:S(2)}) async-start(bf16[384,4,1024]{2,0,1:T(8,128)(2,1)} %fusion), calls=%async_computation.3 | async-start | bytes 6291456 | tf_op jit(solution)/shard_map/all_to_all | solution.py:107
Sparse Core Ops, SparseCore 0:
  10.3 55.5 all-gather.7
  68.1 52.4 all-gather.5
  176.3 76.4 reduce-scatter.9
  254.4 51.7 all-gather.9
  310.3 91.9 reduce-scatter.7
  406.9 91.9 reduce-scatter.5
